TPU v7x, 32 devices: a whole 2x2x4 slice. The times are simulated.
32 devices in a mesh: dp: 8 (over z, x), fsdp: 4 (over y, core).
Axes of the slice: x: 2, y: 2, z: 4, core: 2. Of those that a mesh axis runs over, the one named last changes fastest.
Arguments:
- dec_hidden: bfloat16 [1024, 4096], P('dp'), may hold values from -18 to 18
- w_query: bfloat16 [4096, 2048], P(None, 'fsdp'), may hold values from -0.01171875 to 0.01171875
- enc_states: bfloat16 [2, 1536, 2048], P(None, 'dp', 'fsdp')
- w_out: bfloat16 [2048, 4096], P('fsdp'), may hold values from -0.5 to 0.5
- norm_gain: float32 [4096], replicated, may hold values from 0.25 to 1.75
- w_vocab: bfloat16 [4096, 16384], P(None, 'fsdp'), may hold values from -1 to 1
- enc_segment: int32 [1536], replicated, may hold values from 0 to 3, as said below
- dec_segment: int32 [1024], P('dp'), may hold values from 0 to 3, as said below
- seg_map: int32 [8, 4], replicated, may hold values from 0 to 31, as said below
- targets: int32 [1024], P('dp'), may hold values from 0 to 16383
- loss_mask: int32 [1024], P('dp'), may hold values from 0 to 1, as said below
Outputs:
- mean_loss: float32 [], replicated
- grad_hidden: bfloat16 [1024, 4096], P('dp', 'fsdp')
- grad_gain: float32 [4096], P('fsdp')
Inputs may be any that keep to these rules, and one draw needn't show every extreme that they name: `enc_segment`: each encoder row of 192 tokens holds 4 segments numbered in order, never falling, each nonempty and at most 80 tokens long; one segment of every row is exactly 80 long. `dec_segment`: each decoder row of 128 tokens holds 4 segments numbered in order, never falling, each nonempty and at most 56 tokens long; one segment of every row is exactly 56 long. seg_map[b, j] names the encoder segment (encoder row times 4 plus its number in that row) read by segment j of decoder row b. Every encoder segment is named exactly once. The encoder row read in column j is (b + o_j) mod 8, with offsets o_j that are the same for every decoder row and differ between columns; one of them is 4 and one is 7. The segments of one encoder row go to different decoder rows. `loss_mask`: the first token of every decoder row has mask 1.
All inputs are finite; a program needn't handle non-finite values.
Results may differ from a plain program's by a relative error of at most 0.0086.
Values may be sent and summed in bfloat16 or wider, within the bound.
No kernel may reach another device: no remote copies, remote signals or barrier semaphores. Data moves between devices by JAX's collectives and lax.ppermute only.
A program may use at most 128 MiB of HBM per device.

v0:
```python
import jax
import jax.numpy as jnp
from jax import lax
from jax.sharding import PartitionSpec as P

HEAD_DIM = 64


def joined(x, axis, combine):
    everything = jax.tree.map(lambda part: lax.all_gather(part, axis), x)
    leading = jax.tree.map(lambda part: part[0], everything)

    def turn(k, so_far):
        return combine(so_far, jax.tree.map(lambda part: part[k], everything))

    return lax.fori_loop(1, lax.axis_size(axis), turn, leading)


def merge_totals(first_set, second_set):
    larger = jnp.maximum(first_set[0], second_set[0])
    combined = first_set[1] * jnp.exp(first_set[0] - larger) + second_set[1] * jnp.exp(
        second_set[0] - larger
    )
    return (larger, combined, first_set[2] + second_set[2])


def attend(carry, block, block_ids, queries, sources):
    run_max, run_sum, run_acc = carry
    block_rows = block.shape[1]
    heads_here = queries.shape[1]
    keys_block = block[0].astype(jnp.float32).reshape(block_rows, heads_here, HEAD_DIM)
    values_block = block[1].astype(jnp.float32).reshape(block_rows, heads_here, HEAD_DIM)
    scores = jnp.einsum("ihd,jhd->hij", queries, keys_block)
    allowed = (sources[:, None] == block_ids[None, :])[None]
    new_max = jnp.maximum(run_max, jnp.max(jnp.where(allowed, scores, jnp.float32(-1e30)), 2))
    weights = jnp.where(allowed, jnp.exp(scores - new_max[:, :, None]), 0.0)
    run_sum = jnp.sum(weights, 2)
    run_acc = jnp.einsum("hij,jhd->hid", weights, values_block)
    return (new_max, run_sum, run_acc)


def body(
    dec_hidden,
    w_query,
    enc_states,
    w_out,
    norm_gain,
    w_vocab,
    enc_segment,
    dec_segment,
    seg_map,
    targets,
    loss_mask,
):
    dp_index = lax.axis_index("dp")
    fsdp_index = lax.axis_index("fsdp")
    dp_count = lax.axis_size("dp")
    dec_len, width = dec_hidden.shape
    enc_len = enc_states.shape[1]
    heads_here = w_query.shape[1] // HEAD_DIM
    segments = seg_map.shape[1]
    feature_count = width // lax.axis_size("fsdp")
    vocab_here = w_vocab.shape[1]
    map_row = lax.dynamic_index_in_dim(seg_map, dp_index, 0, keepdims=False)
    segment_picks = dec_segment[:, None] == jnp.arange(segments)[None, :]
    sources = jnp.sum(jnp.where(segment_picks, map_row[None, :], 0), 1)
    query_proj = jnp.dot(dec_hidden, w_query, preferred_element_type=jnp.float32).astype(
        jnp.bfloat16
    )
    queries = (
        lax.optimization_barrier(query_proj)
        .astype(jnp.float32)
        .reshape(dec_len, heads_here, HEAD_DIM)
    )
    start_state = (
        jnp.full((heads_here, dec_len), -1e30, jnp.float32),
        jnp.zeros((heads_here, dec_len), jnp.float32),
        jnp.zeros((heads_here, dec_len, HEAD_DIM), jnp.float32),
    )
    global_ids = jnp.arange(dp_count * enc_len) // enc_len * segments + enc_segment
    state = attend(
        start_state,
        lax.all_gather(enc_states, "dp", axis=1, tiled=True),
        global_ids,
        queries,
        sources,
    )
    run_max, run_sum, run_acc = state
    attended = (
        (run_acc / run_sum[:, :, None])
        .transpose(1, 0, 2)
        .reshape(dec_len, heads_here * HEAD_DIM)
        .astype(jnp.bfloat16)
    )
    feature_start = fsdp_index * feature_count
    gain_part = lax.dynamic_slice_in_dim(norm_gain, feature_start, feature_count, 0)
    summed_full = lax.psum(
        jnp.dot(attended, w_out, preferred_element_type=jnp.float32), "fsdp"
    ) + dec_hidden.astype(jnp.float32)
    inv_root = lax.rsqrt(jnp.sum(summed_full * summed_full, 1) / width + 1e-06)
    unit_full = summed_full * inv_root[:, None]
    normed_full = (unit_full * norm_gain).astype(jnp.bfloat16)
    logits = jnp.dot(normed_full, w_vocab, preferred_element_type=jnp.float32)
    unit_part = lax.dynamic_slice_in_dim(unit_full, feature_start, feature_count, 1)
    local_target = targets - fsdp_index * vocab_here
    picked = jnp.arange(vocab_here)[None, :] == local_target[:, None]
    local_top = jnp.max(logits, 1)
    local_total = jnp.sum(jnp.exp(logits - local_top[:, None]), 1)
    local_pick = jnp.sum(jnp.where(picked, logits, 0.0), 1)
    row_top, row_total, target_logit = joined(
        (local_top, local_total, local_pick), "fsdp", merge_totals
    )
    log_total = row_top + jnp.log(row_total)
    mask_float = loss_mask.astype(jnp.float32)
    grad_logits = (
        mask_float[:, None] * (jnp.exp(logits - log_total[:, None]) - picked.astype(jnp.float32))
    ).astype(jnp.bfloat16)
    grad_normed = lax.psum_scatter(
        lax.dot_general(
            w_vocab, grad_logits, (((1,), (1,)), ((), ())), preferred_element_type=jnp.float32
        ),
        "fsdp",
        scatter_dimension=0,
        tiled=True,
    ).T
    grad_unit = grad_normed * gain_part
    inner_total = lax.psum(jnp.sum(grad_unit * unit_part, 1), "fsdp")
    grad_summed = inv_root[:, None] * (grad_unit - unit_part * (inner_total / width)[:, None])
    gain_local = jnp.sum(grad_normed * unit_part, 0)
    token_count, loss_total, gain_total = lax.psum(
        (jnp.sum(mask_float), jnp.sum(mask_float * (log_total - target_logit)), gain_local), "dp"
    )
    return (
        loss_total / token_count,
        (grad_summed / token_count).astype(jnp.bfloat16),
        gain_total / token_count,
    )


def solution(mesh):
    in_specs = (
        P("dp", None),
        P(None, "fsdp"),
        P(None, "dp", "fsdp"),
        P("fsdp", None),
        P(),
        P(None, "fsdp"),
        P(),
        P("dp"),
        P(),
        P("dp"),
        P("dp"),
    )
    out_specs = (P(), P("dp", "fsdp"), P("fsdp"))
    return jax.shard_map(body, mesh=mesh, in_specs=in_specs, out_specs=out_specs, check_vma=False)
```

profile of v0, /device:TPU:0, one launch (start us, length us, event | category | flops | bytes accessed | tf_op | source)
XLA Modules:
  0.0 266.7 jit_solution(12701368455562883856)
XLA Ops:
  7.2 0.7 all-gather.8.cloned.1.call-update
  8.0 3.2 %convolution_convert_fusion = bf16[128,512]{1,0:T(8,128)(2,1)S(1)} fusion(bf16[128,4096]{1,0:T(8,128)(2,1)} %param.13, bf16[4096,512]{1,0:T(8,128)(2,1)} %param.14), kind=kOutput, calls=%fused_computation.27 | convolution fusion | flops 536936448 | bytes 5373952 | tf_op jit(solution)/shard_map/dot_general | solution.py:67
  11.4 0.2 dynamic-slice_reduce_fusion
  11.7 0.2 broadcast_compare_fusion
  11.8 61.6 %all-gather.8.cloned.1.call-done = bf16[2,1536,512]{2,1,0:T(8,128)(2,1)} async-done(((bf16[2,192,512]{2,1,0:T(8,128)(2,1)}), bf16[2,1536,512]{2,1,0:T(8,128)(2,1)}) %all-gather.8.cloned.1.call-update) | async-done | bytes 3145744 | tf_op jit(solution)/shard_map/all_gather | solution.py:83
  73.4 3.2 %fusion.29 = (bf16[1,1536,512]{2,1,0:T(8,128)(2,1)}, bf16[1,1536,512]{2,1,0:T(8,128)(2,1)S(1)}) fusion(bf16[2,1536,512]{2,1,0:T(8,128)(2,1)} %all-gather.8.cloned.1.call-done), kind=kLoop, calls=%fused_computation.65 | loop fusion | bytes 6291456 | tf_op jit(solution)/shard_map/slice | solution.py:31
  76.6 1.7 copy.24
  78.3 3.8 %select_reduce_fusion = (f32[8,128]{1,0:T(8,128)S(1)}, f32[8,128,1536]{2,1,0:T(8,128)}) fusion(pred[128,1536]{1,0:T(8,128)(4,1)S(1)} %broadcast_compare_fusion, bf16[128,8,64]{0,2,1:T(8,128)(2,1)S(1)} %bitcast.64, bf16[1536,8,64]{0,2,1:T(8,128)(2,1)S(1)} %bitcast.62), kind=kOutput, calls=%fused_computation.11 | convolution fusion | flops 204471296 | bytes 8196096 | tf_op jit(solution)/shard_map/ihd,jhd->hij/dot_general | solution.py:33
  82.1 0.7 copy.25
  82.9 4.3 %fusion.7 = f32[8,128]{1,0:T(8,128)S(1)} fusion(f32[8,128,1536]{2,1,0:T(8,128)} %get-tuple-element.214, f32[8,128]{1,0:T(8,128)S(1)} %broadcast_maximum_fusion, pred[128,1536]{1,0:T(8,128)(4,1)S(1)} %broadcast_compare_fusion), kind=kLoop, calls=%fused_computation.12 | loop fusion | flops 4717568 | bytes 6496256 | tf_op jit(solution)/shard_map/reduce_sum | solution.py:37
  87.1 0.3 copy-done.2
  87.5 1.4 fusion.15
  88.8 0.8 copy-done.7
  89.6 2.0 fusion.31
  91.8 0.6 copy-done.10
  92.3 49.5 %all-reduce.3.cloned.1.call-done = f32[128,4096]{1,0:T(8,128)} async-done(((f32[128,4096]{1,0:T(8,128)}), f32[128,4096]{1,0:T(8,128)}) %all-reduce.3.cloned.1.call-update) | async-done | bytes 2097168 | tf_op jit(solution)/shard_map/psum | solution.py:97
  141.9 2.1 multiply_reduce_fusion
  144.1 0.4 fusion.12
  144.5 0.3 copy-done.8
  144.8 13.7 %fusion.30 = (f32[128]{0:T(128)S(1)}, f32[128,4096]{1,0:T(8,128)S(1)}) fusion(bf16[4096,4096]{1,0:T(8,128)(2,1)} %param.18, f32[128,4096]{1,0:T(8,128)S(1)} %fusion.12, f32[4096]{0:T(1024)S(1)} %copy-done.8), kind=kOutput, calls=%fused_computation.66 | convolution fusion | flops 4296540160 | bytes 37765632 | tf_op jit(solution)/shard_map/dot_general | solution.py:103
  158.6 0.7 select_reduce_fusion.1
  159.3 5.0 %all-gather.5 = f32[4,1,128]{2,1,0:T(1,128)S(1)} all-gather(f32[1,1,128]{2,1,0:T(1,128)S(1)} %bitcast.72), channel_id=4, replica_groups=mesh['dp'=8,'fsdp'=4] {'fsdp'}, dimensions={0}, use_global_device_ids=true | all-gather | bytes 2560 | tf_op jit(solution)/shard_map/all_gather | solution.py:10
  164.3 5.0 %all-gather.4 = f32[4,1,128]{2,1,0:T(1,128)S(1)} all-gather(f32[1,1,128]{2,1,0:T(1,128)S(1)} %bitcast.71), channel_id=3, replica_groups=mesh['dp'=8,'fsdp'=4] {'fsdp'}, dimensions={0}, use_global_device_ids=true | all-gather | bytes 2560 | tf_op jit(solution)/shard_map/all_gather | solution.py:10
  169.3 5.2 %all-gather.3 = f32[4,1,128]{2,1,0:T(1,128)S(1)} all-gather(f32[1,1,128]{2,1,0:T(1,128)S(1)} %bitcast.69), channel_id=2, replica_groups=mesh['dp'=8,'fsdp'=4] {'fsdp'}, dimensions={0}, use_global_device_ids=true | all-gather | bytes 2560 | tf_op jit(solution)/shard_map/all_gather | solution.py:10
  174.7 0.6 convert_reduce_fusion
  175.3 17.3 %convolution_bitcast_fusion = f32[4096,128]{0,1:T(8,128)} fusion(bf16[4096,4096]{1,0:T(8,128)(2,1)} %param.18, f32[128,4096]{1,0:T(8,128)S(1)} %get-tuple-element.216, f32[128]{0:T(128)S(1)} %get-tuple-element.209, f32[128]{0:T(128)S(1)} %convert_element_type.30, s32[128]{0:T(128)S(1)} %broadcast_subtract_fusion), kind=kOutput, calls=%fused_computation.14 | convolution fusion | flops 4298113024 | bytes 37750272 | tf_op jit(solution)/shard_map/dot_general | solution.py:119
  192.6 31.7 %reduce-scatter.2.cloned.1.call-done = f32[1024,128]{0,1:T(8,128)} async-done(((f32[4096,128]{0,1:T(8,128)}), f32[1024,128]{0,1:T(8,128)}) %reduce-scatter.2.cloned.1.call-update) | async-done | bytes 524304 | tf_op jit(solution)/shard_map/reduce_scatter | solution.py:118
  224.3 1.2 fusion.21
  225.5 5.8 %psum.38 = f32[128]{0:T(128)S(1)} all-reduce(f32[128]{0:T(128)S(1)} %get-tuple-element.185), channel_id=1, replica_groups=mesh['dp'=8,'fsdp'=4] {'fsdp'}, use_global_device_ids=true, to_apply=%region_16.17 | all-reduce | flops 128 | bytes 1024 | tf_op jit(solution)/shard_map/psum | solution.py:127
  231.2 22.5 %all-reduce = (f32[]{:T(128)}, f32[]{:T(128)}, f32[1024]{0:T(1024)S(1)}) all-reduce(f32[]{:T(128)} %get-tuple-element.189, f32[]{:T(128)} %get-tuple-element.188, f32[1024]{0:T(1024)S(1)} %get-tuple-element.184), channel_id=1, replica_groups=mesh['dp'=8,'fsdp'=4] {'dp'}, use_global_device_ids=true, to_apply=%region_11.12 | all-reduce | flops 1026 | bytes 8208 | tf_op jit(solution)/shard_map/psum | solution.py:130
  253.8 1.3 broadcast_divide_fusion
  256.4 2.6 divide_convert_fusion
  (43 shorter events, 0.7 us)
Async XLA Ops:
  7.2 4.2 %copy-start = (s32[8,4]{0,1:T(4,128)S(1)}, s32[8,4]{0,1:T(4,128)}, u32[]{:S(2)}) copy-start(s32[8,4]{0,1:T(4,128)} %param.21) | copy-start | bytes 388
  7.2 66.2 %all-gather.8.cloned.1.call-start = ((), (), s32[]{:S(2)}) async-start(), calls=%async_computation.1 | async-start | bytes 3538944 | tf_op jit(solution)/shard_map/all_gather | solution.py:83
  7.9 133.9 %all-reduce.3.cloned.1.call-start = ((), (), s32[]{:S(2)}) async-start(), calls=%async_computation.2 | async-start | bytes 4194304 | tf_op jit(solution)/shard_map/psum | solution.py:97
  8.0 3.6 %copy-start.11 = (s32[128]{0:T(128)S(1)}, s32[128]{0:T(128)}, u32[]{:S(2)}) copy-start(s32[128]{0:T(128)} %param.20) | copy-start | bytes 1540
  8.0 3.7 %copy-start.9 = (s32[1536]{0:T(1024)S(1)}, s32[1536]{0:T(1024)}, u32[]{:S(2)}) copy-start(s32[1536]{0:T(1024)} %param.19) | copy-start | bytes 18436
  82.8 4.6 %copy-start.2 = (f32[8,128,1536]{2,1,0:T(8,128)S(1)}, f32[8,128,1536]{2,1,0:T(8,128)}, u32[]{:S(2)}) copy-start(f32[8,128,1536]{2,1,0:T(8,128)} %get-tuple-element.214) | copy-start | bytes 18874372
  87.4 2.2 copy-start.7
  91.7 0.7 copy-start.10
  91.7 0.7 copy-start.12
  91.7 50.2 %copy-start.5 = (bf16[128,4096]{1,0:T(8,128)(2,1)S(1)}, bf16[128,4096]{1,0:T(8,128)(2,1)}, u32[]{:S(2)}) copy-start(bf16[128,4096]{1,0:T(8,128)(2,1)} %param.13) | copy-start | bytes 3145732
  91.7 132.6 %reduce-scatter.2.cloned.1.call-start = ((), (), s32[]{:S(2)}) async-start(), calls=%async_computation.3 | async-start | bytes 2621440 | tf_op jit(solution)/shard_map/reduce_scatter | solution.py:118
  141.9 2.2 copy-start.6
  144.1 0.7 copy-start.8
  144.8 13.8 %copy-start.3 = (f32[128,4096]{1,0:T(8,128)}, f32[128,4096]{1,0:T(8,128)S(1)}, u32[]{:S(2)}) copy-start(f32[128,4096]{1,0:T(8,128)S(1)} %fusion.12) | copy-start | bytes 6291460
  192.6 31.7 %copy-start.4 = (f32[128,4096]{1,0:T(8,128)S(1)}, f32[128,4096]{1,0:T(8,128)}, u32[]{:S(2)}) copy-start(f32[128,4096]{1,0:T(8,128)} %copy-done.3) | copy-start | bytes 6291460
  192.6 66.5 %copy-start.1 = (s32[8,4]{0,1:T(4,128)S(1)}, s32[8,4]{0,1:T(4,128)}, u32[]{:S(2)}) copy-start(s32[8,4]{0,1:T(4,128)} %param.21) | copy-start | bytes 388
Sparse Core Ops, SparseCore 0:
  10.2 63.1 all-gather.7
  91.8 49.9 all-reduce.2
  192.7 31.5 reduce-scatter.1
where the time goes:
time: 267 us
  waiting for transfers between devices  143 us (54%)
  blocking collectives  43.5 us (16%)
  matrix products  41.5 us (16%)
  between operations  16.4 us (6%)
  other arithmetic  13.6 us (5%)
  local copies, waits for them, and re-layouts  8.11 us (3%)
    all_gather x1, waiting for transfers between devices, body(): lax.all_gather(enc_states, 'dp', axis=1, tiled=True)  61.6 us
    psum x1, waiting for transfers between devices, body(): lax.psum(jnp.dot(attended, w_out, preferred_element_type=jnp.float32), 'f...  49.5 us
    reduce_scatter x1, waiting for transfers between devices, body(): lax.psum_scatter(lax.dot_general(w_vocab, grad_logits, (((1,), (1,)), (()...  31.7 us
    psum x1, blocking collectives, body(): lax.psum((jnp.sum(mask_float), jnp.sum(mask_float * (log_total - target_l...  22.5 us
    dot_general x1, matrix products, body(): lax.dot_general(w_vocab, grad_logits, (((1,), (1,)), ((), ())), preferred...  17.3 us
    all_gather x3, blocking collectives, joined(): everything = jax.tree.map(lambda part: lax.all_gather(part, axis), x)  15.3 us
    dot_general x1, matrix products, body(): logits = jnp.dot(normed_full, w_vocab, preferred_element_type=jnp.float32)  13.7 us
    psum x1, blocking collectives, body(): inner_total = lax.psum(jnp.sum(grad_unit * unit_part, 1), 'fsdp')  5.75 us
  transfers between devices with their start and end apart: 3, of which 3 were waited for; matrix products, arithmetic and copies ran while one was open for 1% of the time, Pallas kernels for 0%

commit v1 on v0

--- a/solution.py
+++ b/solution.py
@@ -4,6 +4,18 @@
 from jax.sharding import PartitionSpec as P
 
 HEAD_DIM = 64
+
+
+def collect(x, axis, dim):
+    ways, here = (lax.axis_size(axis), lax.axis_index(axis))
+    grown, reach = (x, 1)
+    while reach < ways:
+        theirs = lax.ppermute(grown, axis, [(d, d ^ reach) for d in range(ways)])
+        mine_first = jnp.concatenate([grown, theirs], axis=dim)
+        theirs_first = jnp.concatenate([theirs, grown], axis=dim)
+        grown = jnp.where(here & reach == 0, mine_first, theirs_first)
+        reach = 2 * reach
+    return grown
 
 
 def joined(x, axis, combine):
@@ -78,13 +90,7 @@
         jnp.zeros((heads_here, dec_len, HEAD_DIM), jnp.float32),
     )
     global_ids = jnp.arange(dp_count * enc_len) // enc_len * segments + enc_segment
-    state = attend(
-        start_state,
-        lax.all_gather(enc_states, "dp", axis=1, tiled=True),
-        global_ids,
-        queries,
-        sources,
-    )
+    state = attend(start_state, collect(enc_states, "dp", 1), global_ids, queries, sources)
     run_max, run_sum, run_acc = state
     attended = (
         (run_acc / run_sum[:, :, None])

time: 267 us -> 310 us (1.16)
  waiting for transfers between devices: 143 us -> 173 us
  starting transfers between devices: 0.12 us -> 7.56 us
  other arithmetic: 13.6 us -> 19.7 us
    ppermute x0 -> x3, waiting for transfers between devices: none -> 89.6 us  [collect(): theirs = lax.ppermute(grown, axis, [(d, d ^ reach) for d in range(ways)])]
    all_gather x1 -> x0, waiting for transfers between devices: 61.6 us -> none  [body(): lax.all_gather(enc_states, 'dp', axis=1, tiled=True)]
    ppermute x0 -> x3, starting transfers between devices: none -> 7.48 us  [collect(): theirs = lax.ppermute(grown, axis, [(d, d ^ reach) for d in range(ways)])]
    select_n x0 -> x3, other arithmetic: none -> 6.14 us  [collect(): grown = jnp.where(here & reach == 0, mine_first, theirs_first)]
  transfers between devices with their start and end apart: 3 -> 5, of which waited for: 3 -> 5; matrix products, arithmetic and copies ran while one was open for 1% -> 1% of each run, Pallas kernels for 0% -> 0%
where the time goes in v1:
time: 310 us; the launch traced here: 309 us
  waiting for transfers between devices  173 us (56%)
  blocking collectives  43.5 us (14%)
  matrix products  41.2 us (13%)
  other arithmetic  19.7 us (6%)
  between operations  16.7 us (5%)
  local copies, waits for them, and re-layouts  7.76 us (3%)
  starting transfers between devices  7.56 us (2%)
    ppermute x3, waiting for transfers between devices, collect(): theirs = lax.ppermute(grown, axis, [(d, d ^ reach) for d in range(ways)])  89.6 us
    psum x1, waiting for transfers between devices, body(): lax.psum(jnp.dot(attended, w_out, preferred_element_type=jnp.float32), 'f...  51.6 us
    reduce_scatter x1, waiting for transfers between devices, body(): lax.psum_scatter(lax.dot_general(w_vocab, grad_logits, (((1,), (1,)), (()...  31.7 us
    psum x1, blocking collectives, body(): lax.psum((jnp.sum(mask_float), jnp.sum(mask_float * (log_total - target_l...  22.5 us
    dot_general x1, matrix products, body(): lax.dot_general(w_vocab, grad_logits, (((1,), (1,)), ((), ())), preferred...  17.3 us
    all_gather x3, blocking collectives, joined(): everything = jax.tree.map(lambda part: lax.all_gather(part, axis), x)  15.3 us
    dot_general x1, matrix products, body(): logits = jnp.dot(normed_full, w_vocab, preferred_element_type=jnp.float32)  13.7 us
    ppermute x3, starting transfers between devices, collect(): theirs = lax.ppermute(grown, axis, [(d, d ^ reach) for d in range(ways)])  7.48 us
  transfers between devices with their start and end apart: 5, of which 5 were waited for; matrix products, arithmetic and copies ran while one was open for 1% of the time, Pallas kernels for 0%

profile of v1, /device:TPU:0, one launch (start us, length us, event | category | flops | bytes accessed | tf_op | source)
XLA Modules:
  0.0 309.4 jit_solution(2207517145337787555)
XLA Ops:
  7.2 3.0 collective-permute-start
  10.2 9.3 %collective-permute-done = bf16[2,192,512]{2,1,0:T(8,128)(2,1)S(1)} collective-permute-done((bf16[2,192,512]{2,1,0:T(8,128)(2,1)}, bf16[2,192,512]{2,1,0:T(8,128)(2,1)S(1)}, u32[]{:S(2)}, u32[]{:S(2)}) %collective-permute-start) | collective-permute-done | bytes 393248 | tf_op jit(solution)/shard_map/ppermute | solution.py:13
  19.6 1.4 maximum_select_fusion.2
  21.0 1.9 collective-permute-start.1
  22.9 17.0 %collective-permute-done.1 = bf16[2,384,512]{2,1,0:T(8,128)(2,1)} collective-permute-done((bf16[2,384,512]{2,1,0:T(8,128)(2,1)S(1)}, bf16[2,384,512]{2,1,0:T(8,128)(2,1)}, u32[]{:S(2)}, u32[]{:S(2)}) %collective-permute-start.1) | collective-permute-done | bytes 786464 | tf_op jit(solution)/shard_map/ppermute | solution.py:13
  39.9 1.9 maximum_select_fusion.1
  41.8 2.6 collective-permute-start.2
  44.4 3.0 convolution_convert_fusion
  48.0 63.2 %collective-permute-done.2 = bf16[2,768,512]{2,1,0:T(8,128)(2,1)} collective-permute-done((bf16[2,768,512]{2,1,0:T(8,128)(2,1)S(1)}, bf16[2,768,512]{2,1,0:T(8,128)(2,1)}, u32[]{:S(2)}, u32[]{:S(2)}) %collective-permute-start.2) | collective-permute-done | bytes 1572896 | tf_op jit(solution)/shard_map/ppermute | solution.py:13
  111.2 2.8 maximum_select_fusion
  114.0 1.9 fusion.29
  115.9 1.7 copy.24
  117.6 3.8 %select_reduce_fusion = (f32[8,128]{1,0:T(8,128)S(1)}, f32[8,128,1536]{2,1,0:T(8,128)}) fusion(pred[128,1536]{1,0:T(8,128)(4,1)S(1)} %broadcast_compare_fusion, bf16[128,8,64]{0,2,1:T(8,128)(2,1)S(1)} %bitcast.64, bf16[1536,8,64]{0,2,1:T(8,128)(2,1)S(1)} %bitcast.62), kind=kOutput, calls=%fused_computation.11 | convolution fusion | flops 204471296 | bytes 8196096 | tf_op jit(solution)/shard_map/ihd,jhd->hij/dot_general | solution.py:45
  121.4 1.7 copy.25
  123.2 4.3 %fusion.7 = f32[8,128]{1,0:T(8,128)S(1)} fusion(f32[8,128,1536]{2,1,0:T(8,128)} %get-tuple-element.214, f32[8,128]{1,0:T(8,128)S(1)} %broadcast_maximum_fusion, pred[128,1536]{1,0:T(8,128)(4,1)S(1)} %broadcast_compare_fusion), kind=kLoop, calls=%fused_computation.12 | loop fusion | flops 4717568 | bytes 6496256 | tf_op jit(solution)/shard_map/reduce_sum | solution.py:49
  127.7 1.4 fusion.15
  129.1 0.8 copy-done.7
  129.9 2.0 fusion.31
  132.6 51.6 %all-reduce.3.cloned.1.call-done = f32[128,4096]{1,0:T(8,128)} async-done(((f32[128,4096]{1,0:T(8,128)}), f32[128,4096]{1,0:T(8,128)}) %all-reduce.3.cloned.1.call-update) | async-done | bytes 2097168 | tf_op jit(solution)/shard_map/psum | solution.py:103
  184.3 2.1 multiply_reduce_fusion
  187.2 13.7 %fusion.30 = (f32[128]{0:T(128)S(1)}, f32[128,4096]{1,0:T(8,128)S(1)}) fusion(bf16[4096,4096]{1,0:T(8,128)(2,1)} %param.18, f32[128,4096]{1,0:T(8,128)S(1)} %fusion.12, f32[4096]{0:T(1024)S(1)} %copy-done.8), kind=kOutput, calls=%fused_computation.69 | convolution fusion | flops 4296540160 | bytes 37765632 | tf_op jit(solution)/shard_map/dot_general | solution.py:109
  201.0 0.7 select_reduce_fusion.1
  201.7 5.0 %all-gather.5 = f32[4,1,128]{2,1,0:T(1,128)S(1)} all-gather(f32[1,1,128]{2,1,0:T(1,128)S(1)} %bitcast.72), channel_id=4, replica_groups=mesh['dp'=8,'fsdp'=4] {'fsdp'}, dimensions={0}, use_global_device_ids=true | all-gather | bytes 2560 | tf_op jit(solution)/shard_map/all_gather | solution.py:22
  206.7 5.0 %all-gather.4 = f32[4,1,128]{2,1,0:T(1,128)S(1)} all-gather(f32[1,1,128]{2,1,0:T(1,128)S(1)} %bitcast.71), channel_id=3, replica_groups=mesh['dp'=8,'fsdp'=4] {'fsdp'}, dimensions={0}, use_global_device_ids=true | all-gather | bytes 2560 | tf_op jit(solution)/shard_map/all_gather | solution.py:22
  211.8 5.2 %all-gather.3 = f32[4,1,128]{2,1,0:T(1,128)S(1)} all-gather(f32[1,1,128]{2,1,0:T(1,128)S(1)} %bitcast.69), channel_id=2, replica_groups=mesh['dp'=8,'fsdp'=4] {'fsdp'}, dimensions={0}, use_global_device_ids=true | all-gather | bytes 2560 | tf_op jit(solution)/shard_map/all_gather | solution.py:22
  217.7 17.3 %convolution_bitcast_fusion = f32[4096,128]{0,1:T(8,128)} fusion(bf16[4096,4096]{1,0:T(8,128)(2,1)} %param.18, f32[128,4096]{1,0:T(8,128)S(1)} %get-tuple-element.216, f32[128]{0:T(128)S(1)} %get-tuple-element.209, f32[128]{0:T(128)S(1)} %convert_element_type.30, s32[128]{0:T(128)S(1)} %broadcast_subtract_fusion), kind=kOutput, calls=%fused_computation.14 | convolution fusion | flops 4298113024 | bytes 37750272 | tf_op jit(solution)/shard_map/dot_general | solution.py:125
  235.0 31.7 %reduce-scatter.2.cloned.1.call-done = f32[1024,128]{0,1:T(8,128)} async-done(((f32[4096,128]{0,1:T(8,128)}), f32[1024,128]{0,1:T(8,128)}) %reduce-scatter.2.cloned.1.call-update) | async-done | bytes 524304 | tf_op jit(solution)/shard_map/reduce_scatter | solution.py:124
  266.7 1.2 fusion.21
  267.9 5.8 %psum.38 = f32[128]{0:T(128)S(1)} all-reduce(f32[128]{0:T(128)S(1)} %get-tuple-element.185), channel_id=1, replica_groups=mesh['dp'=8,'fsdp'=4] {'fsdp'}, use_global_device_ids=true, to_apply=%region_16.17 | all-reduce | flops 128 | bytes 1024 | tf_op jit(solution)/shard_map/psum | solution.py:133
  273.7 22.5 %all-reduce = (f32[]{:T(128)}, f32[]{:T(128)}, f32[1024]{0:T(1024)S(1)}) all-reduce(f32[]{:T(128)} %get-tuple-element.189, f32[]{:T(128)} %get-tuple-element.188, f32[1024]{0:T(1024)S(1)} %get-tuple-element.184), channel_id=1, replica_groups=mesh['dp'=8,'fsdp'=4] {'dp'}, use_global_device_ids=true, to_apply=%region_11.12 | all-reduce | flops 1026 | bytes 8208 | tf_op jit(solution)/shard_map/psum | solution.py:136
  296.2 1.3 broadcast_divide_fusion
  298.8 2.6 divide_convert_fusion
  (49 shorter events, 3.3 us)
Async XLA Ops:
  7.2 40.3 %copy-start = (s32[8,4]{0,1:T(4,128)S(1)}, s32[8,4]{0,1:T(4,128)}, u32[]{:S(2)}) copy-start(s32[8,4]{0,1:T(4,128)} %param.21) | copy-start | bytes 388
  7.2 177.1 %all-reduce.3.cloned.1.call-start = ((), (), s32[]{:S(2)}) async-start(), calls=%async_computation.1 | async-start | bytes 4194304 | tf_op jit(solution)/shard_map/psum | solution.py:103
  7.2 12.3 %collective-permute-start = (bf16[2,192,512]{2,1,0:T(8,128)(2,1)}, bf16[2,192,512]{2,1,0:T(8,128)(2,1)S(1)}, u32[]{:S(2)}, u32[]{:S(2)}) collective-permute-start(bf16[2,192,512]{2,1,0:T(8,128)(2,1)} %param.15), channel_id=1, source_target_pairs={{0,4},{4,0},{8,12},{12,8},{16,20},{20,16},{24,28},{28,24},{1,5},{5... | collective-permute-start | bytes 1179656 | tf_op jit(solution)/shard_map/ppermute | solution.py:13
  10.2 34.1 %copy-start.5 = (bf16[128,4096]{1,0:T(8,128)(2,1)S(1)}, bf16[128,4096]{1,0:T(8,128)(2,1)}, u32[]{:S(2)}) copy-start(bf16[128,4096]{1,0:T(8,128)(2,1)} %param.13) | copy-start | bytes 3145732
  21.0 18.9 %collective-permute-start.1 = (bf16[2,384,512]{2,1,0:T(8,128)(2,1)S(1)}, bf16[2,384,512]{2,1,0:T(8,128)(2,1)}, u32[]{:S(2)}, u32[]{:S(2)}) collective-permute-start(bf16[2,384,512]{2,1,0:T(8,128)(2,1)S(1)} %maximum_select_fusion.2), channel_id=1, source_target_pairs={{0,8},{4,12},{8,0},{12,4},{16,24},{20,28},{24,16},{28,20},{1,9},{5... | collective-permute-start | bytes 2359304 | tf_op jit(solution)/shard_map/ppermute | solution.py:13
  41.8 69.4 %collective-permute-start.2 = (bf16[2,768,512]{2,1,0:T(8,128)(2,1)S(1)}, bf16[2,768,512]{2,1,0:T(8,128)(2,1)}, u32[]{:S(2)}, u32[]{:S(2)}) collective-permute-start(bf16[2,768,512]{2,1,0:T(8,128)(2,1)S(1)} %maximum_select_fusion.1), channel_id=1, source_target_pairs={{0,16},{4,20},{8,24},{12,28},{16,0},{20,4},{24,8},{28,12},{1,17},{... | collective-permute-start | bytes 4718600 | tf_op jit(solution)/shard_map/ppermute | solution.py:13
  44.4 3.3 %copy-start.11 = (s32[128]{0:T(128)S(1)}, s32[128]{0:T(128)}, u32[]{:S(2)}) copy-start(s32[128]{0:T(128)} %param.20) | copy-start | bytes 1540
  44.4 3.4 %copy-start.9 = (s32[1536]{0:T(1024)S(1)}, s32[1536]{0:T(1024)}, u32[]{:S(2)}) copy-start(s32[1536]{0:T(1024)} %param.19) | copy-start | bytes 18436
  123.1 4.6 %copy-start.2 = (f32[8,128,1536]{2,1,0:T(8,128)S(1)}, f32[8,128,1536]{2,1,0:T(8,128)}, u32[]{:S(2)}) copy-start(f32[8,128,1536]{2,1,0:T(8,128)} %get-tuple-element.214) | copy-start | bytes 18874372
  127.7 2.2 copy-start.7
  132.0 0.7 copy-start.10
  132.0 0.7 copy-start.12
  132.0 134.7 %reduce-scatter.2.cloned.1.call-start = ((), (), s32[]{:S(2)}) async-start(), calls=%async_computation.2 | async-start | bytes 2621440 | tf_op jit(solution)/shard_map/reduce_scatter | solution.py:124
  184.3 2.2 copy-start.6
  186.5 0.7 copy-start.8
  187.2 13.8 %copy-start.3 = (f32[128,4096]{1,0:T(8,128)}, f32[128,4096]{1,0:T(8,128)S(1)}, u32[]{:S(2)}) copy-start(f32[128,4096]{1,0:T(8,128)S(1)} %fusion.12) | copy-start | bytes 6291460
  235.0 31.7 %copy-start.4 = (f32[128,4096]{1,0:T(8,128)S(1)}, f32[128,4096]{1,0:T(8,128)}, u32[]{:S(2)}) copy-start(f32[128,4096]{1,0:T(8,128)} %copy-done.3) | copy-start | bytes 6291460
  235.0 66.4 %copy-start.1 = (s32[8,4]{0,1:T(4,128)S(1)}, s32[8,4]{0,1:T(4,128)}, u32[]{:S(2)}) copy-start(s32[8,4]{0,1:T(4,128)} %param.21) | copy-start | bytes 388
Sparse Core Ops, SparseCore 0:
  132.1 52.1 all-reduce.2
  235.1 31.5 reduce-scatter.1
